TPU v7x, 128 devices: a whole 4x4x4 slice. The times are simulated.
128 devices in a mesh: seq: 32 (over y, x, z_lo), chan: 4 (over z_hi, core).
Axes of the slice: x: 4, y: 4, z: 4 (z_hi: 2, z_lo: 2; z = z_hi * 2 + z_lo), core: 2. Of those that a mesh axis runs over, the one named last changes fastest.
Arguments:
- tokens: bfloat16 [24576, 4096], P('seq', 'chan'), may hold values from -4 to 4
- w_in: bfloat16 [8, 4096, 1296], P('chan', 'seq'), may hold values from -1 to 1
- conv_w: float32 [8, 4, 1280], P('chan'), may hold values from -3 to 3
- conv_b: float32 [8, 1280], P('chan'), may hold values from -3 to 3
- dt_bias: float32 [8, 16], P('chan'), may hold values from -8 to 2
- a_log: float32 [8, 16], P('chan'), may hold values from -4.6 to -3.7
- d_skip: float32 [8, 16], P('chan'), may hold values from 0.3 to 3
- norm_gain: float32 [8, 1024], P('chan'), may hold values from 0.5 to 1.5
Outputs:
- mixer_out: bfloat16 [24576, 8192], P('seq', 'chan')
All inputs are finite; a program needn't handle non-finite values.
Results may differ from a plain program's by a relative error of at most 0.0076.
Values may be sent and summed in bfloat16 or wider, within the bound.
No kernel may reach another device: no remote copies, remote signals or barrier semaphores. Data moves between devices by JAX's collectives and lax.ppermute only.
A program may use at most 128 MiB of HBM per device.

v0:
```python
import jax
import jax.numpy as jnp
from jax import lax
from jax.sharding import Mesh, PartitionSpec as P

P_SIZE = 64
N = 128
KCONV = 4
Q = 128
HG = 16
GW = 1024
CW = 1280
epsilon = 1e-05
SEQ = "seq"


def shifted(block, axis, distance):
    devices = range(lax.axis_size(axis))
    route = [(i - distance, i) for i in devices if i - distance in devices]
    return lax.ppermute(block, axis, route)


def combine(earlier, later):
    return (earlier[0] * later[0], later[0][..., None, None] * earlier[1] + later[1])


def gather_level(own, axis, need_total):
    size = lax.axis_size(axis)
    place = lax.axis_index(axis)
    groups, heads = own[0].shape
    shape = own[1].shape
    tail = shape[-1]
    rows = own[1].reshape(groups, -1, tail)
    keep_rows = jnp.pad(own[0][:, None, :], ((0, 0), (0, 7), (0, tail - heads)))
    packed = jnp.concatenate([rows, keep_rows], axis=1)
    body = rows.shape[1]
    received = [None]
    for distance in range(1, size):
        if need_total:
            route = [(i, (i + distance) % size) for i in range(size)]
        else:
            route = [(i, i + distance) for i in range(size - distance)]
        got = lax.ppermute(packed, axis, route)
        received.append((got[:, body, :heads], got[:, :body].reshape(shape)))
    prefix = (jnp.ones_like(own[0]), jnp.zeros_like(own[1]))
    for distance in range(size - 1, 0, -1):
        joined = combine(prefix, received[distance])
        reach = distance <= place
        prefix = (jnp.where(reach, joined[0], prefix[0]), jnp.where(reach, joined[1], prefix[1]))
    if not need_total:
        return (prefix, None)
    total = combine(prefix, own)
    for distance in range(size - 1, 0, -1):
        joined = combine(total, received[distance])
        beyond = distance > place
        total = (jnp.where(beyond, joined[0], total[0]), jnp.where(beyond, joined[1], total[1]))
    return (prefix, total)


def entering(keep, end, axes):
    carried = (keep, end)
    prefixes = []
    for level, axis in enumerate(reversed(axes)):
        prefix, carried = gather_level(carried, axis, level < len(axes) - 1)
        prefixes.append(prefix)
    result = prefixes[-1]
    for prefix in reversed(prefixes[:-1]):
        result = combine(result, prefix)
    return result[1]


def mix_groups(gathered, w_in, conv_w, conv_b, dt_bias, a_log, d_skip, norm_gain, after):
    groups = w_in.shape[0]
    row_count = gathered.shape[0]
    rows_first = jnp.transpose(w_in, (1, 0, 2))
    if isinstance(SEQ, tuple):
        pair = lax.axis_size(SEQ[2])
        slot = lax.axis_index(SEQ[2])
        piece = rows_first.shape[0]
        pair_w = jnp.zeros((piece * pair,) + rows_first.shape[1:], rows_first.dtype)
        for distance in range(pair):
            if distance:
                rows = lax.ppermute(
                    rows_first, SEQ[2], [(i, (i + distance) % pair) for i in range(pair)]
                )
            else:
                rows = rows_first
            source = (slot - distance) % pair
            pair_w = lax.dynamic_update_slice(pair_w, rows, (source * piece, 0, 0))
        full_w = lax.all_gather(pair_w, SEQ[:2], axis=0, tiled=True)
    else:
        full_w = lax.all_gather(rows_first, SEQ, axis=0, tiled=True)
    if after is not None:
        full_w, _ = lax.optimization_barrier((full_w, after))
    projected = jnp.einsum("td,dgc->tgc", gathered, full_w, preferred_element_type=jnp.float32)
    conv_in = projected[:, :, :CW].astype(jnp.bfloat16)
    raw_dt = projected[:, :, CW:]
    rim_rows = shifted(conv_in[row_count - (KCONV - 1) :], SEQ, 1)
    padded = jnp.concatenate([rim_rows, conv_in], axis=0)
    pre_act = jnp.broadcast_to(conv_b[None], (row_count, groups, CW))
    for offset in range(KCONV):
        pre_act = pre_act + conv_w[None, :, offset] * padded[offset : offset + row_count]
    inputs = jax.nn.silu(pre_act).astype(jnp.bfloat16)
    block_count = row_count // Q
    blocked = inputs.reshape(block_count, Q, groups, CW)
    x_all = blocked[..., :GW].reshape(block_count, Q, groups, HG, P_SIZE)
    b_all = blocked[..., GW : GW + N]
    c_all = blocked[..., GW + N :]
    step_dt = jax.nn.softplus(raw_dt + dt_bias[None]).reshape(block_count, Q, groups, HG)
    decay_rate = -jnp.exp(a_log)
    cumulative = jnp.cumsum(decay_rate[None, None] * step_dt, axis=1)
    causal = lax.broadcasted_iota(jnp.int32, (Q, Q), 0) >= lax.broadcasted_iota(
        jnp.int32, (Q, Q), 1
    )
    last_cum = cumulative[:, -1]
    keep_all = jnp.exp(last_cum)
    tail_factor = jnp.exp(last_cum[:, None] - cumulative) * step_dt
    scaled = (x_all * tail_factor[..., None]).astype(jnp.bfloat16)
    fresh_all = jnp.einsum("qjghp,qjgn->qghpn", scaled, b_all, preferred_element_type=jnp.float32)
    local_states = []
    state_now = jnp.zeros(fresh_all.shape[1:], jnp.float32)
    keep_now = jnp.ones(keep_all.shape[1:], jnp.float32)
    keep_before = []
    for q in range(block_count):
        local_states.append(state_now)
        keep_before.append(keep_now)
        state_now = keep_all[q][..., None, None] * state_now + fresh_all[q]
        keep_now = keep_now * keep_all[q]
    incoming = entering(keep_now, state_now, SEQ if isinstance(SEQ, tuple) else (SEQ,))
    states = jnp.stack(local_states) + jnp.stack(keep_before)[..., None, None] * incoming[None]
    scores = jnp.einsum("qign,qjgn->qgij", c_all, b_all, preferred_element_type=jnp.float32)
    cum_cols = jnp.transpose(cumulative, (0, 2, 3, 1))
    dt_cols = jnp.transpose(step_dt, (0, 2, 3, 1))
    spread = cum_cols[..., :, None] - cum_cols[..., None, :]
    damping = jnp.where(causal, jnp.exp(jnp.minimum(spread, 0.0)), 0.0)
    weights = (scores[:, :, None] * damping * dt_cols[..., None, :]).astype(jnp.bfloat16)
    partial_y = jnp.einsum("qghij,qjghp->qighp", weights, x_all, preferred_element_type=jnp.float32)
    partial_y = partial_y + d_skip[None, None, :, :, None] * x_all
    across = jnp.einsum(
        "qign,qghpn->qighp", c_all, states.astype(jnp.bfloat16), preferred_element_type=jnp.float32
    )
    activity = partial_y + jnp.exp(cumulative)[..., None] * across
    flat_act = activity.reshape(row_count, groups, GW)
    inv_rms = lax.rsqrt(jnp.mean(flat_act * flat_act, axis=-1, keepdims=True) + epsilon)
    normed = (flat_act * inv_rms * norm_gain[None]).astype(jnp.bfloat16)
    return (normed.reshape(row_count, groups * GW), state_now)


def per_device(tokens, w_in, conv_w, conv_b, dt_bias, a_log, d_skip, norm_gain):
    size = lax.axis_size("chan")
    place = lax.axis_index("chan")
    width = tokens.shape[1]
    gathered = jnp.zeros((tokens.shape[0], width * size), tokens.dtype)
    for distance in range(size):
        if distance:
            piece = lax.ppermute(tokens, "chan", [(i, (i + distance) % size) for i in range(size)])
        else:
            piece = tokens
        source = (place - distance) % size
        gathered = lax.dynamic_update_slice(gathered, piece, (0, source * width))
    outputs = []
    after = None
    for g in range(w_in.shape[0]):
        one = slice(g, g + 1)
        normed, after = mix_groups(
            gathered,
            w_in[one],
            conv_w[one],
            conv_b[one],
            dt_bias[one],
            a_log[one],
            d_skip[one],
            norm_gain[one],
            after,
        )
        outputs.append(normed)
    return jnp.concatenate(outputs, axis=1)


def split_mesh(mesh):
    global SEQ
    devices = mesh.devices
    try:
        flat = devices.reshape(-1)
        across_y = len({d.coords[1] for d in flat})
        across_x = len({d.coords[0] for d in flat})
    except (AttributeError, IndexError, TypeError):
        SEQ = "seq"
        return mesh
    seq_size, chan_size = devices.shape
    if seq_size % (across_y * across_x) or across_y * across_x == seq_size:
        SEQ = "seq"
        return mesh
    pair = seq_size // (across_y * across_x)
    SEQ = ("y", "x", "zl")
    return Mesh(devices.reshape(across_y, across_x, pair, chan_size), SEQ + ("chan",))


def solution(mesh):
    mesh = split_mesh(mesh)
    return jax.shard_map(
        per_device,
        mesh=mesh,
        in_specs=(
            P(SEQ, "chan"),
            P("chan", SEQ, None),
            P("chan", None, None),
            P("chan", None),
            P("chan", None),
            P("chan", None),
            P("chan", None),
            P("chan", None),
        ),
        out_specs=P(SEQ, "chan"),
        check_vma=False,
    )
```

profile of v0, /device:TPU:22, one launch (start us, length us, event | category | flops | bytes accessed | tf_op | source)
XLA Modules:
  0.0 387.2 jit_solution(5249604030271814485)
XLA Ops:
  10.8 6.7 %collective-permute-done.3 = bf16[128,1,1296]{0,2,1:T(8,128)(2,1)S(1)} collective-permute-done((bf16[128,1,1296]{0,2,1:T(8,128)(2,1)S(1)}, bf16[128,1,1296]{0,2,1:T(8,128)(2,1)S(1)}, u32[]{:S(2)}, u32[]{:S(2)}) %collective-permute-start.3) | collective-permute-done | bytes 331808 | tf_op jit(solution)/shard_map/ppermute | solution.py:83
  20.5 7.0 %collective-permute-done.12 = bf16[128,1,1296]{0,2,1:T(8,128)(2,1)S(1)} collective-permute-done((bf16[128,1,1296]{0,2,1:T(8,128)(2,1)S(1)}, bf16[128,1,1296]{0,2,1:T(8,128)(2,1)S(1)}, u32[]{:S(2)}, u32[]{:S(2)}) %collective-permute-start.12) | collective-permute-done | bytes 331808 | tf_op jit(solution)/shard_map/ppermute | solution.py:83
  28.5 3.6 collective-permute-start.1
  39.6 3.5 broadcast_in_dim.20
  46.7 19.7 %collective-permute-done = bf16[768,1024]{1,0:T(8,128)(2,1)} collective-permute-done((bf16[768,1024]{1,0:T(8,128)(2,1)}, bf16[768,1024]{1,0:T(8,128)(2,1)}, u32[]{:S(2)}, u32[]{:S(2)}) %collective-permute-start) | collective-permute-done | bytes 1572896 | tf_op jit(solution)/shard_map/ppermute | solution.py:156
  70.4 29.8 %collective-permute-done.2 = bf16[768,1024]{1,0:T(8,128)(2,1)S(1)} collective-permute-done((bf16[768,1024]{1,0:T(8,128)(2,1)}, bf16[768,1024]{1,0:T(8,128)(2,1)S(1)}, u32[]{:S(2)}, u32[]{:S(2)}) %collective-permute-start.2) | collective-permute-done | bytes 1572896 | tf_op jit(solution)/shard_map/ppermute | solution.py:156
  101.5 6.8 %all-gather.3.cloned.1.call-done = bf16[4096,1,1296]{0,2,1:T(8,128)(2,1)} async-done(((bf16[256,1,1296]{0,2,1:T(8,128)(2,1)}), bf16[4096,1,1296]{0,2,1:T(8,128)(2,1)}) %all-gather.3.cloned.1.call-update) | async-done | bytes 10616848 | tf_op jit(solution)/shard_map/all_gather | solution.py:90
  108.3 13.0 %fusion.85 = (bf16[768,1,1296]{0,2,1:T(8,128)(2,1)S(1)}, f32[768,1,1296]{0,2,1:T(8,128)S(1)}) fusion(bf16[768,4096]{1,0:T(8,128)(2,1)} %constant_dynamic-update-slice_fusion.24, bf16[4096,1,1296]{0,2,1:T(8,128)(2,1)} %all-gather.3.cloned.1.call-done), kind=kOutput, calls=%fused_computation.268 | convolution fusion | flops 8154722304 | bytes 22880256 | tf_op jit(solution)/shard_map/td,dgc->tgc/dot_general | solution.py:95
  121.7 3.9 %collective-permute-start.4 = (bf16[3,1,1280]{0,2,1:T(8,128)(2,1)S(1)}, bf16[3,1,1280]{0,2,1:T(8,128)(2,1)S(1)}, u32[]{:S(2)}, u32[]{:S(2)}) collective-permute-start(bf16[3,1,1280]{0,2,1:T(8,128)(2,1)S(1)} %slice.454), channel_id=1, source_target_pairs={{0,4},{4,8},{8,12},{12,16},{16,20},{20,24},{24,28},{28,32},{32,36}... | collective-permute-start | bytes 23048 | tf_op jit(solution)/shard_map/ppermute | solution.py:20
  134.1 4.8 %collective-permute-done.4 = bf16[3,1,1280]{0,2,1:T(8,128)(2,1)S(1)} collective-permute-done((bf16[3,1,1280]{0,2,1:T(8,128)(2,1)S(1)}, bf16[3,1,1280]{0,2,1:T(8,128)(2,1)S(1)}, u32[]{:S(2)}, u32[]{:S(2)}) %collective-permute-start.4) | collective-permute-done | bytes 7712 | tf_op jit(solution)/shard_map/ppermute | solution.py:20
  138.9 6.1 %multiply_convert_fusion.3 = bf16[768,1,1280]{0,2,1:T(8,128)(2,1)} fusion(bf16[768,1,1280]{0,2,1:T(8,128)(2,1)S(1)} %slice.455, bf16[3,1,1280]{0,2,1:T(8,128)(2,1)S(1)} %collective-permute-done.4, f32[1280]{0:T(1024)} %get-tuple-element.9, f32[1280]{0:T(1024)} %get-tuple-element.10, f32[1280]{0:T(1024)} %get-tuple-element.11, f32[1280]{0:T(1024)} %get-tuple-element.12, ...), kind=kLoop, calls=%fused_computation.7 | loop fusion | flops 25559040 | bytes 3965440 | tf_op jit(solution)/shard_map/convert_element_type | solution.py:103
  145.0 4.0 %copy.54 = bf16[768,1,1280]{2,0,1:T(8,128)(2,1)} copy(bf16[768,1,1280]{0,2,1:T(8,128)(2,1)} %multiply_convert_fusion.3) | data formatting | bytes 3932160 | tf_op jit(solution)/shard_map/convert_element_type | solution.py:103
  149.0 3.1 slice_convert_fusion.1
  163.9 38.9 %all-gather.5.cloned.1.call-done = bf16[4096,1,1296]{0,2,1:T(8,128)(2,1)} async-done(((bf16[256,1,1296]{0,2,1:T(8,128)(2,1)}), bf16[4096,1,1296]{0,2,1:T(8,128)(2,1)}) %all-gather.5.cloned.1.call-update) | async-done | bytes 10616848 | tf_op jit(solution)/shard_map/all_gather | solution.py:90
  202.8 14.0 %fusion.86 = (bf16[768,1,1296]{0,2,1:T(8,128)(2,1)}, f32[768,1,1296]{0,2,1:T(8,128)S(1)}) fusion(bf16[768,4096]{1,0:T(8,128)(2,1)} %constant_dynamic-update-slice_fusion.24, bf16[4096,1,1296]{0,2,1:T(8,128)(2,1)} %all-gather.5.cloned.1.call-done), kind=kOutput, calls=%fused_computation.269 | convolution fusion | flops 8154722304 | bytes 22880256 | tf_op jit(solution)/shard_map/td,dgc->tgc/dot_general | solution.py:95
  236.2 5.6 %fusion.10 = f32[6,16,64,128]{3,2,1,0:T(8,128)} fusion(bf16[6,128,16,64]{1,3,2,0:T(8,128)(2,1)} %bitcast.427, f32[6,16,128]{2,1,0:T(8,128)} %copy.59, f32[6,16,128]{2,1,0:T(8,128)} %copy.57, f32[6,128,128]{2,1,0:T(8,128)} %fusion.51, pred[128,128]{1,0:T(8,128)(4,1)} %iota_compare_fusion.1), kind=kOutput, calls=%fused_computation.10 | convolution fusion | flops 210763776 | bytes 5226496 | tf_op jit(solution)/shard_map/qghij,qjghp->qighp/dot_general | solution.py:137
  249.6 10.0 %multiply_convert_fusion.2 = bf16[768,1,1280]{0,2,1:T(8,128)(2,1)} fusion(bf16[768,1,1280]{0,2,1:T(8,128)(2,1)} %slice.492, bf16[3,1,1280]{0,2,1:T(8,128)(2,1)} %collective-permute-done.13, f32[1280]{0:T(1024)} %get-tuple-element.13, f32[1280]{0:T(1024)} %get-tuple-element.14, f32[1280]{0:T(1024)} %get-tuple-element.8, f32[1280]{0:T(1024)} %get-tuple-element.7, ...), kind=kLoop, calls=%fused_computation.6 | loop fusion | flops 25559040 | bytes 3965440 | tf_op jit(solution)/shard_map/convert_element_type | solution.py:103
  271.4 3.6 collective-permute-start.14
  275.9 3.6 copy.70
  279.5 5.2 %fusion.11 = f32[6,16,64,128]{3,2,1,0:T(8,128)S(1)} fusion(bf16[6,128,16,64]{1,3,2,0:T(8,128)(2,1)} %bitcast.429, f32[6,16,128]{2,1,0:T(8,128)} %copy.69, f32[6,16,128]{2,1,0:T(8,128)} %copy.67, f32[6,128,128]{2,1,0:T(8,128)S(1)} %copy-done.19, pred[128,128]{1,0:T(8,128)(4,1)} %iota_compare_fusion.1), kind=kOutput, calls=%fused_computation.11 | convolution fusion | flops 210763776 | bytes 5226496 | tf_op jit(solution)/shard_map/qghij,qjghp->qighp/dot_general | solution.py:137
  297.5 18.1 %collective-permute-done.6 = f32[1,1032,128]{2,1,0:T(8,128)S(1)} collective-permute-done((f32[1,1032,128]{2,1,0:T(8,128)S(1)}, f32[1,1032,128]{2,1,0:T(8,128)S(1)}, u32[]{:S(2)}, u32[]{:S(2)}) %collective-permute-start.6) | collective-permute-done | bytes 528416 | tf_op jit(solution)/shard_map/ppermute | solution.py:43
  319.1 16.3 %collective-permute-done.15 = f32[1,1032,128]{2,1,0:T(8,128)S(1)} collective-permute-done((f32[1,1032,128]{2,1,0:T(8,128)S(1)}, f32[1,1032,128]{2,1,0:T(8,128)S(1)}, u32[]{:S(2)}, u32[]{:S(2)}) %collective-permute-start.15) | collective-permute-done | bytes 528416 | tf_op jit(solution)/shard_map/ppermute | solution.py:43
  340.1 16.6 %collective-permute-start.18 = (f32[1,1032,128]{2,1,0:T(8,128)S(1)}, f32[1,1032,128]{2,1,0:T(8,128)S(1)}, u32[]{:S(2)}, u32[]{:S(2)}) collective-permute-start(f32[1,1032,128]{2,1,0:T(8,128)S(1)} %select_maximum_fusion), channel_id=1, source_target_pairs={{0,32},{32,64},{64,96},{1,33},{33,65},{65,97},{2,34},{34,66},{66,9... | collective-permute-start | bytes 1585160 | tf_op jit(solution)/shard_map/ppermute | solution.py:43
  356.9 6.0 %collective-permute-done.9 = f32[1,1032,128]{2,1,0:T(8,128)S(1)} collective-permute-done((f32[1,1032,128]{2,1,0:T(8,128)S(1)}, f32[1,1032,128]{2,1,0:T(8,128)S(1)}, u32[]{:S(2)}, u32[]{:S(2)}) %collective-permute-start.9) | collective-permute-done | bytes 528416 | tf_op jit(solution)/shard_map/ppermute | solution.py:43
  (272 shorter events, 122.5 us)
Async XLA Ops:
  6.5 29.0 %copy-start.23 = (f32[2,4,1280]{2,1,0:T(4,128)S(1)}, f32[2,4,1280]{2,1,0:T(4,128)}, u32[]{:S(2)}) copy-start(f32[2,4,1280]{2,1,0:T(4,128)} %param.10) | copy-start | bytes 122884
  6.5 101.8 %all-gather.3.cloned.1.call-start = ((), (), s32[]{:S(2)}) async-start(), calls=%async_computation | async-start | bytes 11280384 | tf_op jit(solution)/shard_map/all_gather | solution.py:90
  7.7 9.8 %collective-permute-start.3 = (bf16[128,1,1296]{0,2,1:T(8,128)(2,1)S(1)}, bf16[128,1,1296]{0,2,1:T(8,128)(2,1)S(1)}, u32[]{:S(2)}, u32[]{:S(2)}) collective-permute-start(bf16[128,1,1296]{0,2,1:T(8,128)(2,1)S(1)} %get-tuple-element.39), channel_id=1, source_target_pairs={{0,4},{4,0},{1,5},{5,1},{2,6},{6,2},{3,7},{7,3},{8,12},{12,8},{9,1... | collective-permute-start | bytes 995336 | tf_op jit(solution)/shard_map/ppermute | solution.py:83
  18.5 184.3 %all-gather.5.cloned.1.call-start = ((), (), s32[]{:S(2)}) async-start(), calls=%async_computation.1 | async-start | bytes 11280384 | tf_op jit(solution)/shard_map/all_gather | solution.py:90
  18.5 8.9 %collective-permute-start.12 = (bf16[128,1,1296]{0,2,1:T(8,128)(2,1)S(1)}, bf16[128,1,1296]{0,2,1:T(8,128)(2,1)S(1)}, u32[]{:S(2)}, u32[]{:S(2)}) collective-permute-start(bf16[128,1,1296]{0,2,1:T(8,128)(2,1)S(1)} %get-tuple-element.40), channel_id=1, source_target_pairs={{0,4},{4,0},{1,5},{5,1},{2,6},{6,2},{3,7},{7,3},{8,12},{12,8},{9,1... | collective-permute-start | bytes 995336 | tf_op jit(solution)/shard_map/ppermute | solution.py:83
  28.4 38.0 %collective-permute-start = (bf16[768,1024]{1,0:T(8,128)(2,1)}, bf16[768,1024]{1,0:T(8,128)(2,1)}, u32[]{:S(2)}, u32[]{:S(2)}) collective-permute-start(bf16[768,1024]{1,0:T(8,128)(2,1)} %param.8), channel_id=1, source_target_pairs={{0,1},{1,2},{2,3},{3,0},{4,5},{5,6},{6,7},{7,4},{8,9},{9,10},{10,1... | collective-permute-start | bytes 4718600 | tf_op jit(solution)/shard_map/ppermute | solution.py:156
  28.5 40.6 %collective-permute-start.1 = (bf16[768,1024]{1,0:T(8,128)(2,1)}, bf16[768,1024]{1,0:T(8,128)(2,1)S(1)}, u32[]{:S(2)}, u32[]{:S(2)}) collective-permute-start(bf16[768,1024]{1,0:T(8,128)(2,1)} %param.8), channel_id=1, source_target_pairs={{0,2},{1,3},{2,0},{3,1},{4,6},{5,7},{6,4},{7,5},{8,10},{9,11},{10,... | collective-permute-start | bytes 4718600 | tf_op jit(solution)/shard_map/ppermute | solution.py:156
  32.1 68.1 %collective-permute-start.2 = (bf16[768,1024]{1,0:T(8,128)(2,1)}, bf16[768,1024]{1,0:T(8,128)(2,1)S(1)}, u32[]{:S(2)}, u32[]{:S(2)}) collective-permute-start(bf16[768,1024]{1,0:T(8,128)(2,1)} %param.8), channel_id=1, source_target_pairs={{0,3},{1,0},{2,1},{3,2},{4,7},{5,4},{6,5},{7,6},{8,11},{9,8},{10,9... | collective-permute-start | bytes 4718600 | tf_op jit(solution)/shard_map/ppermute | solution.py:156
  121.7 17.3 %collective-permute-start.4 = (bf16[3,1,1280]{0,2,1:T(8,128)(2,1)S(1)}, bf16[3,1,1280]{0,2,1:T(8,128)(2,1)S(1)}, u32[]{:S(2)}, u32[]{:S(2)}) collective-permute-start(bf16[3,1,1280]{0,2,1:T(8,128)(2,1)S(1)} %slice.454), channel_id=1, source_target_pairs={{0,4},{4,8},{8,12},{12,16},{16,20},{20,24},{24,28},{28,32},{32,36}... | collective-permute-start | bytes 23048 | tf_op jit(solution)/shard_map/ppermute | solution.py:20
  224.5 60.3 %collective-permute-start.5 = (f32[1,1032,128]{2,1,0:T(8,128)}, f32[1,1032,128]{2,1,0:T(8,128)}, u32[]{:S(2)}, u32[]{:S(2)}) collective-permute-start(f32[1,1032,128]{2,1,0:T(8,128)} %select_maximum_fusion.5), channel_id=1, source_target_pairs={{0,4},{4,0},{1,5},{5,1},{2,6},{6,2},{3,7},{7,3},{8,12},{12,8},{9,1... | collective-permute-start | bytes 1585160 | tf_op jit(solution)/shard_map/ppermute | solution.py:43
  227.9 21.6 %collective-permute-start.13 = (bf16[3,1,1280]{0,2,1:T(8,128)(2,1)}, bf16[3,1,1280]{0,2,1:T(8,128)(2,1)}, u32[]{:S(2)}, u32[]{:S(2)}) collective-permute-start(bf16[3,1,1280]{0,2,1:T(8,128)(2,1)} %slice.491), channel_id=1, source_target_pairs={{0,4},{4,8},{8,12},{12,16},{16,20},{20,24},{24,28},{28,32},{32,36}... | collective-permute-start | bytes 23048 | tf_op jit(solution)/shard_map/ppermute | solution.py:20
  271.4 20.1 %collective-permute-start.14 = (f32[1,1032,128]{2,1,0:T(8,128)}, f32[1,1032,128]{2,1,0:T(8,128)}, u32[]{:S(2)}, u32[]{:S(2)}) collective-permute-start(f32[1,1032,128]{2,1,0:T(8,128)} %select_maximum_fusion.2), channel_id=1, source_target_pairs={{0,4},{4,0},{1,5},{5,1},{2,6},{6,2},{3,7},{7,3},{8,12},{12,8},{9,1... | collective-permute-start | bytes 1585160 | tf_op jit(solution)/shard_map/ppermute | solution.py:43
  288.1 27.6 %collective-permute-start.6 = (f32[1,1032,128]{2,1,0:T(8,128)S(1)}, f32[1,1032,128]{2,1,0:T(8,128)S(1)}, u32[]{:S(2)}, u32[]{:S(2)}) collective-permute-start(f32[1,1032,128]{2,1,0:T(8,128)S(1)} %select_maximum_fusion.4), channel_id=1, source_target_pairs={{0,24},{8,0},{16,8},{24,16},{1,25},{9,1},{17,9},{25,17},{2,26},{10... | collective-permute-start | bytes 1585160 | tf_op jit(solution)/shard_map/ppermute | solution.py:43
  288.2 27.5 %collective-permute-start.7 = (f32[1,1032,128]{2,1,0:T(8,128)S(1)}, f32[1,1032,128]{2,1,0:T(8,128)S(1)}, u32[]{:S(2)}, u32[]{:S(2)}) collective-permute-start(f32[1,1032,128]{2,1,0:T(8,128)S(1)} %select_maximum_fusion.4), channel_id=1, source_target_pairs={{0,16},{8,24},{16,0},{24,8},{1,17},{9,25},{17,1},{25,9},{2,18},{10... | collective-permute-start | bytes 1585160 | tf_op jit(solution)/shard_map/ppermute | solution.py:43
  289.0 27.5 %collective-permute-start.8 = (f32[1,1032,128]{2,1,0:T(8,128)S(1)}, f32[1,1032,128]{2,1,0:T(8,128)S(1)}, u32[]{:S(2)}, u32[]{:S(2)}) collective-permute-start(f32[1,1032,128]{2,1,0:T(8,128)S(1)} %select_maximum_fusion.4), channel_id=1, source_target_pairs={{0,8},{8,16},{16,24},{24,0},{1,9},{9,17},{17,25},{25,1},{2,10},{10... | collective-permute-start | bytes 1585160 | tf_op jit(solution)/shard_map/ppermute | solution.py:43
  294.3 41.2 %collective-permute-start.15 = (f32[1,1032,128]{2,1,0:T(8,128)S(1)}, f32[1,1032,128]{2,1,0:T(8,128)S(1)}, u32[]{:S(2)}, u32[]{:S(2)}) collective-permute-start(f32[1,1032,128]{2,1,0:T(8,128)S(1)} %select_maximum_fusion.1), channel_id=1, source_target_pairs={{0,24},{8,0},{16,8},{24,16},{1,25},{9,1},{17,9},{25,17},{2,26},{10... | collective-permute-start | bytes 1585160 | tf_op jit(solution)/shard_map/ppermute | solution.py:43
  295.2 42.2 %collective-permute-start.16 = (f32[1,1032,128]{2,1,0:T(8,128)S(1)}, f32[1,1032,128]{2,1,0:T(8,128)S(1)}, u32[]{:S(2)}, u32[]{:S(2)}) collective-permute-start(f32[1,1032,128]{2,1,0:T(8,128)S(1)} %select_maximum_fusion.1), channel_id=1, source_target_pairs={{0,16},{8,24},{16,0},{24,8},{1,17},{9,25},{17,1},{25,9},{2,18},{10... | collective-permute-start | bytes 1585160 | tf_op jit(solution)/shard_map/ppermute | solution.py:43
  315.7 21.7 %collective-permute-start.17 = (f32[1,1032,128]{2,1,0:T(8,128)S(1)}, f32[1,1032,128]{2,1,0:T(8,128)S(1)}, u32[]{:S(2)}, u32[]{:S(2)}) collective-permute-start(f32[1,1032,128]{2,1,0:T(8,128)S(1)} %select_maximum_fusion.1), channel_id=1, source_target_pairs={{0,8},{8,16},{16,24},{24,0},{1,9},{9,17},{17,25},{25,1},{2,10},{10... | collective-permute-start | bytes 1585160 | tf_op jit(solution)/shard_map/ppermute | solution.py:43
  317.1 22.9 %collective-permute-start.11 = (f32[1,1032,128]{2,1,0:T(8,128)S(1)}, f32[1,1032,128]{2,1,0:T(8,128)S(1)}, u32[]{:S(2)}, u32[]{:S(2)}) collective-permute-start(f32[1,1032,128]{2,1,0:T(8,128)S(1)} %select_maximum_fusion.3), channel_id=1, source_target_pairs={{0,96},{1,97},{2,98},{3,99},{4,100},{5,101},{6,102},{7,103},{8,104... | collective-permute-start | bytes 1585160 | tf_op jit(solution)/shard_map/ppermute | solution.py:43
  317.8 39.0 %collective-permute-start.10 = (f32[1,1032,128]{2,1,0:T(8,128)S(1)}, f32[1,1032,128]{2,1,0:T(8,128)S(1)}, u32[]{:S(2)}, u32[]{:S(2)}) collective-permute-start(f32[1,1032,128]{2,1,0:T(8,128)S(1)} %select_maximum_fusion.3), channel_id=1, source_target_pairs={{0,64},{32,96},{1,65},{33,97},{2,66},{34,98},{3,67},{35,99},{4,68}... | collective-permute-start | bytes 1585160 | tf_op jit(solution)/shard_map/ppermute | solution.py:43
  335.4 27.5 %collective-permute-start.9 = (f32[1,1032,128]{2,1,0:T(8,128)S(1)}, f32[1,1032,128]{2,1,0:T(8,128)S(1)}, u32[]{:S(2)}, u32[]{:S(2)}) collective-permute-start(f32[1,1032,128]{2,1,0:T(8,128)S(1)} %select_maximum_fusion.3), channel_id=1, source_target_pairs={{0,32},{32,64},{64,96},{1,33},{33,65},{65,97},{2,34},{34,66},{66,9... | collective-permute-start | bytes 1585160 | tf_op jit(solution)/shard_map/ppermute | solution.py:43
  338.0 32.1 %collective-permute-start.20 = (f32[1,1032,128]{2,1,0:T(8,128)S(1)}, f32[1,1032,128]{2,1,0:T(8,128)S(1)}, u32[]{:S(2)}, u32[]{:S(2)}) collective-permute-start(f32[1,1032,128]{2,1,0:T(8,128)S(1)} %select_maximum_fusion), channel_id=1, source_target_pairs={{0,96},{1,97},{2,98},{3,99},{4,100},{5,101},{6,102},{7,103},{8,104... | collective-permute-start | bytes 1585160 | tf_op jit(solution)/shard_map/ppermute | solution.py:43
  338.7 31.5 %collective-permute-start.19 = (f32[1,1032,128]{2,1,0:T(8,128)S(1)}, f32[1,1032,128]{2,1,0:T(8,128)S(1)}, u32[]{:S(2)}, u32[]{:S(2)}) collective-permute-start(f32[1,1032,128]{2,1,0:T(8,128)S(1)} %select_maximum_fusion), channel_id=1, source_target_pairs={{0,64},{32,96},{1,65},{33,97},{2,66},{34,98},{3,67},{35,99},{4,68}... | collective-permute-start | bytes 1585160 | tf_op jit(solution)/shard_map/ppermute | solution.py:43
  340.1 30.2 %collective-permute-start.18 = (f32[1,1032,128]{2,1,0:T(8,128)S(1)}, f32[1,1032,128]{2,1,0:T(8,128)S(1)}, u32[]{:S(2)}, u32[]{:S(2)}) collective-permute-start(f32[1,1032,128]{2,1,0:T(8,128)S(1)} %select_maximum_fusion), channel_id=1, source_target_pairs={{0,32},{32,64},{64,96},{1,33},{33,65},{65,97},{2,34},{34,66},{66,9... | collective-permute-start | bytes 1585160 | tf_op jit(solution)/shard_map/ppermute | solution.py:43
  (51 other events, 259.1 us)
Sparse Core Ops, SparseCore 0:
  18.6 89.6 all-gather.2
  110.4 92.3 all-gather.4
where the time goes:
time: 394 us; the launch traced here: 387 us
  waiting for transfers between devices  155 us (39%)
  local copies, waits for them, and re-layouts  67 us (17%)
  starting transfers between devices  50.9 us (13%)
  matrix products  50.1 us (13%)
  other arithmetic  49.5 us (13%)
  between operations  14.7 us (4%)
    ppermute x3, waiting for transfers between devices, per_device(): lax.ppermute(tokens, 'chan', [(i, (i + distance) % size) for i in range(s...  49.4 us
    all_gather x2, waiting for transfers between devices, mix_groups(): full_w = lax.all_gather(pair_w, SEQ[:2], axis=0, tiled=True)  45.7 us
    ppermute x14, waiting for transfers between devices, gather_level(): got = lax.ppermute(packed, axis, route)  41.3 us
    ppermute x14, starting transfers between devices, gather_level(): got = lax.ppermute(packed, axis, route)  34.1 us
    dot_general x2, matrix products, mix_groups(): jnp.einsum('td,dgc->tgc', gathered, full_w, preferred_element_type=jnp.fl...  27 us
    convert_element_type x2, other arithmetic, mix_groups(): inputs = jax.nn.silu(pre_act).astype(jnp.bfloat16)  16.1 us
    ppermute x2, waiting for transfers between devices, mix_groups(): lax.ppermute(rows_first, SEQ[2], [(i, (i + distance) % pair) for i in ran...  13.7 us
    dot_general x2, matrix products, mix_groups(): jnp.einsum('qghij,qjghp->qighp', weights, x_all, preferred_element_type=j...  10.8 us
  transfers between devices with their start and end apart: 23, of which 11 were waited for; matrix products, arithmetic and copies ran while one was open for 34% of the time, Pallas kernels for 0%

commit v1 on v0

--- a/solution.py
+++ b/solution.py
@@ -87,7 +87,9 @@
                 rows = rows_first
             source = (slot - distance) % pair
             pair_w = lax.dynamic_update_slice(pair_w, rows, (source * piece, 0, 0))
-        full_w = lax.all_gather(pair_w, SEQ[:2], axis=0, tiled=True)
+        full_w = jnp.concatenate(
+            lax.all_to_all(jnp.stack([pair_w] * lax.axis_size(SEQ[:2])), SEQ[:2], 0, 0), axis=0
+        )
     else:
         full_w = lax.all_gather(rows_first, SEQ, axis=0, tiled=True)
     if after is not None:

time: 394 us -> 551 us (1.40)
  waiting for transfers between devices: 155 us -> 298 us
  local copies, waits for them, and re-layouts: 67 us -> 89.1 us
  starting transfers between devices: 50.9 us -> 68.2 us
  between operations: 14.7 us -> 1.55 us
  matrix products: 50.1 us -> 43.1 us
    all_to_all x0 -> x2, waiting for transfers between devices: none -> 197 us  [mix_groups(): lax.all_to_all(jnp.stack([pair_w] * lax.axis_size(SEQ[:2])), SEQ[:2], 0, 0)]
    all_gather x2 -> x0, waiting for transfers between devices: 45.7 us -> none  [mix_groups(): full_w = lax.all_gather(pair_w, SEQ[:2], axis=0, tiled=True)]
    all_to_all x0 -> x2, starting transfers between devices: none -> 14.4 us  [mix_groups(): lax.all_to_all(jnp.stack([pair_w] * lax.axis_size(SEQ[:2])), SEQ[:2], 0, 0)]
    reshape x0 -> x1, local copies, waits for them, and re-layouts: none -> 10.1 us  [mix_groups(): jnp.concatenate(lax.all_to_all(jnp.stack([pair_w] * lax.axis_size(SEQ[:2]...]
    another operation x2, local copies, waits for them, and re-layouts: 0.09 us -> 9.34 us  [mix_groups(): jnp.stack([pair_w] * lax.axis_size(SEQ[:2]))]
    unnamed x116 -> x135, local copies, waits for them, and re-layouts: 10.3 us -> 18.4 us
    ppermute x14, waiting for transfers between devices: 41.3 us -> 35.1 us  [gather_level(): got = lax.ppermute(packed, axis, route)]
    dot_general x2, matrix products: 27 us -> 21 us  [mix_groups(): jnp.einsum('td,dgc->tgc', gathered, full_w, preferred_element_type=jnp.fl...]
  transfers between devices with their start and end apart: 23 -> 23, of which waited for: 11 -> 11; matrix products, arithmetic and copies ran while one was open for 34% -> 21% of each run, Pallas kernels for 0% -> 0%
where the time goes in v1:
time: 551 us; the launch traced here: 545 us
  waiting for transfers between devices  298 us (54%)
  local copies, waits for them, and re-layouts  89.1 us (16%)
  starting transfers between devices  68.2 us (12%)
  other arithmetic  45.2 us (8%)
  matrix products  43.1 us (8%)
    all_to_all x2, waiting for transfers between devices, mix_groups(): lax.all_to_all(jnp.stack([pair_w] * lax.axis_size(SEQ[:2])), SEQ[:2], 0, 0)  197 us
    ppermute x3, waiting for transfers between devices, per_device(): lax.ppermute(tokens, 'chan', [(i, (i + distance) % size) for i in range(s...  53.1 us
    ppermute x14, starting transfers between devices, gather_level(): got = lax.ppermute(packed, axis, route)  36.7 us
    ppermute x14, waiting for transfers between devices, gather_level(): got = lax.ppermute(packed, axis, route)  35.1 us
    dot_general x2, matrix products, mix_groups(): jnp.einsum('td,dgc->tgc', gathered, full_w, preferred_element_type=jnp.fl...  21 us
    unnamed x135, local copies, waits for them, and re-layouts  18.4 us
    convert_element_type x2, other arithmetic, mix_groups(): inputs = jax.nn.silu(pre_act).astype(jnp.bfloat16)  15.4 us
    all_to_all x2, starting transfers between devices, mix_groups(): lax.all_to_all(jnp.stack([pair_w] * lax.axis_size(SEQ[:2])), SEQ[:2], 0, 0)  14.4 us
  transfers between devices with their start and end apart: 23, of which 11 were waited for; matrix products, arithmetic and copies ran while one was open for 21% of the time, Pallas kernels for 0%

profile of v1, /device:TPU:22, one launch (start us, length us, event | category | flops | bytes accessed | tf_op | source)
XLA Modules:
  0.0 545.1 jit_solution(1463268173706752860)
XLA Ops:
  4.2 6.7 %collective-permute-done.3 = bf16[128,1,1296]{0,2,1:T(8,128)(2,1)S(1)} collective-permute-done((bf16[128,1,1296]{0,2,1:T(8,128)(2,1)S(1)}, bf16[128,1,1296]{0,2,1:T(8,128)(2,1)S(1)}, u32[]{:S(2)}, u32[]{:S(2)}) %collective-permute-start.3) | collective-permute-done | bytes 331808 | tf_op jit(solution)/shard_map/ppermute | solution.py:83
  11.0 4.7 stack.14
  15.7 7.3 %all-to-all-start = ((bf16[16,256,1,1296]{1,3,2,0:T(8,128)(2,1)}), bf16[16,256,1,1296]{1,3,2,0:T(8,128)(2,1)}, u32[]{:S(2)}, u32[]{:S(2)}) async-start(bf16[16,256,1,1296]{1,3,2,0:T(8,128)(2,1)} %stack.14), calls=%async_computation | async-start | bytes 21233664 | tf_op jit(solution)/shard_map/all_to_all | solution.py:91
  24.9 6.4 %collective-permute-done.12 = bf16[128,1,1296]{0,2,1:T(8,128)(2,1)S(1)} collective-permute-done((bf16[128,1,1296]{0,2,1:T(8,128)(2,1)S(1)}, bf16[128,1,1296]{0,2,1:T(8,128)(2,1)S(1)}, u32[]{:S(2)}, u32[]{:S(2)}) %collective-permute-start.12) | collective-permute-done | bytes 331808 | tf_op jit(solution)/shard_map/ppermute | solution.py:83
  31.4 145.6 %all-to-all-done = bf16[16,256,1,1296]{1,3,2,0:T(8,128)(2,1)} async-done(((bf16[16,256,1,1296]{1,3,2,0:T(8,128)(2,1)}), bf16[16,256,1,1296]{1,3,2,0:T(8,128)(2,1)}, u32[]{:S(2)}, u32[]{:S(2)}) %all-to-all-start) | async-done | bytes 10616864 | tf_op jit(solution)/shard_map/all_to_all | solution.py:91
  177.1 4.6 stack.18
  181.7 7.1 %all-to-all-start.1 = ((bf16[16,256,1,1296]{1,3,2,0:T(8,128)(2,1)}), bf16[16,256,1,1296]{1,3,2,0:T(8,128)(2,1)}, u32[]{:S(2)}, u32[]{:S(2)}) async-start(bf16[16,256,1,1296]{1,3,2,0:T(8,128)(2,1)} %stack.18), calls=%async_computation.1 | async-start | bytes 21233664 | tf_op jit(solution)/shard_map/all_to_all | solution.py:91
  203.6 22.9 %collective-permute-done = bf16[768,1024]{1,0:T(8,128)(2,1)} collective-permute-done((bf16[768,1024]{1,0:T(8,128)(2,1)S(1)}, bf16[768,1024]{1,0:T(8,128)(2,1)}, u32[]{:S(2)}, u32[]{:S(2)}) %collective-permute-start) | collective-permute-done | bytes 1572896 | tf_op jit(solution)/shard_map/ppermute | solution.py:158
  229.8 30.2 %collective-permute-done.2 = bf16[768,1024]{1,0:T(8,128)(2,1)S(1)} collective-permute-done((bf16[768,1024]{1,0:T(8,128)(2,1)S(1)}, bf16[768,1024]{1,0:T(8,128)(2,1)S(1)}, u32[]{:S(2)}, u32[]{:S(2)}) %collective-permute-start.2) | collective-permute-done | bytes 1572896 | tf_op jit(solution)/shard_map/ppermute | solution.py:158
  260.2 7.6 %copy.114 = bf16[162,8,16,256]{3,1,2,0:T(8,128)(2,1)S(1)} copy(bf16[162,8,16,256]{3,1,0,2:T(8,128)(2,1)} %bitcast.378) | data formatting | bytes 21233664
  267.8 8.8 %fusion.80 = (bf16[768,1,1296]{0,2,1:T(8,128)(2,1)S(1)}, f32[768,1,1296]{0,2,1:T(8,128)S(1)}) fusion(bf16[768,4096]{1,0:T(8,128)(2,1)S(1)} %constant_dynamic-update-slice_fusion.20, bf16[4096,1296]{0,1:T(8,128)(2,1)S(1)} %bitcast.425), kind=kOutput, calls=%fused_computation.266 | convolution fusion | flops 8154722304 | bytes 22880256 | tf_op jit(solution)/shard_map/td,dgc->tgc/dot_general | solution.py:97
  288.9 51.0 %all-to-all-done.1 = bf16[16,256,1,1296]{1,3,2,0:T(8,128)(2,1)} async-done(((bf16[16,256,1,1296]{1,3,2,0:T(8,128)(2,1)}), bf16[16,256,1,1296]{1,3,2,0:T(8,128)(2,1)}, u32[]{:S(2)}, u32[]{:S(2)}) %all-to-all-start.1) | async-done | bytes 10616864 | tf_op jit(solution)/shard_map/all_to_all | solution.py:91
  340.0 10.1 %copy.113 = bf16[16,1,162,8,256]{4,3,0,2,1:T(8,128)(2,1)} copy(bf16[16,1,162,8,256]{4,3,2,1,0:T(8,128)(2,1)} %bitcast.137) | data formatting | bytes 21233664 | tf_op jit(solution)/shard_map/reshape | solution.py:90
  350.2 5.2 multiply_convert_fusion.3
  355.4 4.0 copy.83
  373.4 12.2 %fusion.81 = (bf16[768,1,1296]{0,2,1:T(8,128)(2,1)}, f32[768,1,1296]{0,2,1:T(8,128)S(1)}) fusion(bf16[768,4096]{1,0:T(8,128)(2,1)S(1)} %bitcast.435, bf16[4096,1,1296]{0,2,1:T(8,128)(2,1)} %bitcast.424), kind=kOutput, calls=%fused_computation.267 | convolution fusion | flops 8154722304 | bytes 22880256 | tf_op jit(solution)/shard_map/td,dgc->tgc/dot_general | solution.py:97
  405.0 5.6 %fusion.5 = f32[6,16,64,128]{3,2,1,0:T(8,128)} fusion(bf16[6,128,16,64]{1,3,2,0:T(8,128)(2,1)} %bitcast.437, f32[6,16,128]{2,1,0:T(8,128)} %copy.88, f32[6,16,128]{2,1,0:T(8,128)} %copy.86, f32[6,128,128]{2,1,0:T(8,128)} %fusion.46, pred[128,128]{1,0:T(8,128)(4,1)} %iota_compare_fusion.1), kind=kOutput, calls=%fused_computation.8 | convolution fusion | flops 210763776 | bytes 5226496 | tf_op jit(solution)/shard_map/qghij,qjghp->qighp/dot_general | solution.py:139
  418.4 10.2 %multiply_convert_fusion.2 = bf16[768,1,1280]{0,2,1:T(8,128)(2,1)} fusion(bf16[768,1,1280]{0,2,1:T(8,128)(2,1)} %slice.492, bf16[3,1,1280]{0,2,1:T(8,128)(2,1)} %collective-permute-done.13, f32[1280]{0:T(1024)} %get-tuple-element.13, f32[1280]{0:T(1024)} %get-tuple-element.14, f32[1280]{0:T(1024)} %get-tuple-element.8, f32[1280]{0:T(1024)} %get-tuple-element.7, ...), kind=kLoop, calls=%fused_computation.4 | loop fusion | flops 25559040 | bytes 3965440 | tf_op jit(solution)/shard_map/convert_element_type | solution.py:105
  440.4 6.1 %collective-permute-start.14 = (f32[1,1032,128]{2,1,0:T(8,128)}, f32[1,1032,128]{2,1,0:T(8,128)}, u32[]{:S(2)}, u32[]{:S(2)}) collective-permute-start(f32[1,1032,128]{2,1,0:T(8,128)} %select_maximum_fusion.2), channel_id=1, source_target_pairs={{0,4},{4,0},{1,5},{5,1},{2,6},{6,2},{3,7},{7,3},{8,12},{12,8},{9,1... | collective-permute-start | bytes 1585160 | tf_op jit(solution)/shard_map/ppermute | solution.py:43
  451.0 5.2 fusion.6
  469.0 18.1 %collective-permute-done.6 = f32[1,1032,128]{2,1,0:T(8,128)S(1)} collective-permute-done((f32[1,1032,128]{2,1,0:T(8,128)S(1)}, f32[1,1032,128]{2,1,0:T(8,128)S(1)}, u32[]{:S(2)}, u32[]{:S(2)}) %collective-permute-start.6) | collective-permute-done | bytes 528416 | tf_op jit(solution)/shard_map/ppermute | solution.py:43
  490.6 10.6 %collective-permute-done.15 = f32[1,1032,128]{2,1,0:T(8,128)S(1)} collective-permute-done((f32[1,1032,128]{2,1,0:T(8,128)S(1)}, f32[1,1032,128]{2,1,0:T(8,128)S(1)}, u32[]{:S(2)}, u32[]{:S(2)}) %collective-permute-start.15) | collective-permute-done | bytes 528416 | tf_op jit(solution)/shard_map/ppermute | solution.py:43
  506.0 17.5 %collective-permute-start.18 = (f32[1,1032,128]{2,1,0:T(8,128)S(1)}, f32[1,1032,128]{2,1,0:T(8,128)S(1)}, u32[]{:S(2)}, u32[]{:S(2)}) collective-permute-start(f32[1,1032,128]{2,1,0:T(8,128)S(1)} %select_maximum_fusion), channel_id=1, source_target_pairs={{0,32},{32,64},{64,96},{1,33},{33,65},{65,97},{2,34},{34,66},{66,9... | collective-permute-start | bytes 1585160 | tf_op jit(solution)/shard_map/ppermute | solution.py:43
  523.6 3.8 collective-permute-done.9
  (293 shorter events, 132.0 us)
Async XLA Ops:
  1.1 9.8 %collective-permute-start.3 = (bf16[128,1,1296]{0,2,1:T(8,128)(2,1)S(1)}, bf16[128,1,1296]{0,2,1:T(8,128)(2,1)S(1)}, u32[]{:S(2)}, u32[]{:S(2)}) collective-permute-start(bf16[128,1,1296]{0,2,1:T(8,128)(2,1)S(1)} %get-tuple-element.39), channel_id=1, source_target_pairs={{0,4},{4,0},{1,5},{5,1},{2,6},{6,2},{3,7},{7,3},{8,12},{12,8},{9,1... | collective-permute-start | bytes 995336 | tf_op jit(solution)/shard_map/ppermute | solution.py:83
  15.7 161.3 %all-to-all-start = ((bf16[16,256,1,1296]{1,3,2,0:T(8,128)(2,1)}), bf16[16,256,1,1296]{1,3,2,0:T(8,128)(2,1)}, u32[]{:S(2)}, u32[]{:S(2)}) async-start(bf16[16,256,1,1296]{1,3,2,0:T(8,128)(2,1)} %stack.14), calls=%async_computation | async-start | bytes 21233664 | tf_op jit(solution)/shard_map/all_to_all | solution.py:91
  23.1 8.3 %collective-permute-start.12 = (bf16[128,1,1296]{0,2,1:T(8,128)(2,1)S(1)}, bf16[128,1,1296]{0,2,1:T(8,128)(2,1)S(1)}, u32[]{:S(2)}, u32[]{:S(2)}) collective-permute-start(bf16[128,1,1296]{0,2,1:T(8,128)(2,1)S(1)} %get-tuple-element.40), channel_id=1, source_target_pairs={{0,4},{4,0},{1,5},{5,1},{2,6},{6,2},{3,7},{7,3},{8,12},{12,8},{9,1... | collective-permute-start | bytes 995336 | tf_op jit(solution)/shard_map/ppermute | solution.py:83
  181.7 158.3 %all-to-all-start.1 = ((bf16[16,256,1,1296]{1,3,2,0:T(8,128)(2,1)}), bf16[16,256,1,1296]{1,3,2,0:T(8,128)(2,1)}, u32[]{:S(2)}, u32[]{:S(2)}) async-start(bf16[16,256,1,1296]{1,3,2,0:T(8,128)(2,1)} %stack.18), calls=%async_computation.1 | async-start | bytes 21233664 | tf_op jit(solution)/shard_map/all_to_all | solution.py:91
  188.8 37.7 %collective-permute-start = (bf16[768,1024]{1,0:T(8,128)(2,1)S(1)}, bf16[768,1024]{1,0:T(8,128)(2,1)}, u32[]{:S(2)}, u32[]{:S(2)}) collective-permute-start(bf16[768,1024]{1,0:T(8,128)(2,1)S(1)} %copy-done.18), channel_id=1, source_target_pairs={{0,1},{1,2},{2,3},{3,0},{4,5},{5,6},{6,7},{7,4},{8,9},{9,10},{10,1... | collective-permute-start | bytes 4718600 | tf_op jit(solution)/shard_map/ppermute | solution.py:158
  188.9 39.3 %collective-permute-start.1 = (bf16[768,1024]{1,0:T(8,128)(2,1)S(1)}, bf16[768,1024]{1,0:T(8,128)(2,1)}, u32[]{:S(2)}, u32[]{:S(2)}) collective-permute-start(bf16[768,1024]{1,0:T(8,128)(2,1)S(1)} %copy-done.18), channel_id=1, source_target_pairs={{0,2},{1,3},{2,0},{3,1},{4,6},{5,7},{6,4},{7,5},{8,10},{9,11},{10,... | collective-permute-start | bytes 4718600 | tf_op jit(solution)/shard_map/ppermute | solution.py:158
  192.1 67.8 %collective-permute-start.2 = (bf16[768,1024]{1,0:T(8,128)(2,1)S(1)}, bf16[768,1024]{1,0:T(8,128)(2,1)S(1)}, u32[]{:S(2)}, u32[]{:S(2)}) collective-permute-start(bf16[768,1024]{1,0:T(8,128)(2,1)S(1)} %copy-done.18), channel_id=1, source_target_pairs={{0,3},{1,0},{2,1},{3,2},{4,7},{5,4},{6,5},{7,6},{8,11},{9,8},{10,9... | collective-permute-start | bytes 4718600 | tf_op jit(solution)/shard_map/ppermute | solution.py:158
  276.9 73.2 %collective-permute-start.4 = (bf16[3,1,1280]{0,2,1:T(8,128)(2,1)S(1)}, bf16[3,1,1280]{0,2,1:T(8,128)(2,1)S(1)}, u32[]{:S(2)}, u32[]{:S(2)}) collective-permute-start(bf16[3,1,1280]{0,2,1:T(8,128)(2,1)S(1)} %slice.454), channel_id=1, source_target_pairs={{0,4},{4,8},{8,12},{12,16},{16,20},{20,24},{24,28},{28,32},{32,36}... | collective-permute-start | bytes 23048 | tf_op jit(solution)/shard_map/ppermute | solution.py:20
  393.4 62.8 %collective-permute-start.5 = (f32[1,1032,128]{2,1,0:T(8,128)}, f32[1,1032,128]{2,1,0:T(8,128)}, u32[]{:S(2)}, u32[]{:S(2)}) collective-permute-start(f32[1,1032,128]{2,1,0:T(8,128)} %select_maximum_fusion.5), channel_id=1, source_target_pairs={{0,4},{4,0},{1,5},{5,1},{2,6},{6,2},{3,7},{7,3},{8,12},{12,8},{9,1... | collective-permute-start | bytes 1585160 | tf_op jit(solution)/shard_map/ppermute | solution.py:43
  396.1 22.3 %collective-permute-start.13 = (bf16[3,1,1280]{0,2,1:T(8,128)(2,1)}, bf16[3,1,1280]{0,2,1:T(8,128)(2,1)}, u32[]{:S(2)}, u32[]{:S(2)}) collective-permute-start(bf16[3,1,1280]{0,2,1:T(8,128)(2,1)} %slice.491), channel_id=1, source_target_pairs={{0,4},{4,8},{8,12},{12,16},{16,20},{20,24},{24,28},{28,32},{32,36}... | collective-permute-start | bytes 23048 | tf_op jit(solution)/shard_map/ppermute | solution.py:20
  440.4 22.5 %collective-permute-start.14 = (f32[1,1032,128]{2,1,0:T(8,128)}, f32[1,1032,128]{2,1,0:T(8,128)}, u32[]{:S(2)}, u32[]{:S(2)}) collective-permute-start(f32[1,1032,128]{2,1,0:T(8,128)} %select_maximum_fusion.2), channel_id=1, source_target_pairs={{0,4},{4,0},{1,5},{5,1},{2,6},{6,2},{3,7},{7,3},{8,12},{12,8},{9,1... | collective-permute-start | bytes 1585160 | tf_op jit(solution)/shard_map/ppermute | solution.py:43
  459.6 27.6 %collective-permute-start.6 = (f32[1,1032,128]{2,1,0:T(8,128)S(1)}, f32[1,1032,128]{2,1,0:T(8,128)S(1)}, u32[]{:S(2)}, u32[]{:S(2)}) collective-permute-start(f32[1,1032,128]{2,1,0:T(8,128)S(1)} %select_maximum_fusion.4), channel_id=1, source_target_pairs={{0,24},{8,0},{16,8},{24,16},{1,25},{9,1},{17,9},{25,17},{2,26},{10... | collective-permute-start | bytes 1585160 | tf_op jit(solution)/shard_map/ppermute | solution.py:43
  459.7 27.5 %collective-permute-start.7 = (f32[1,1032,128]{2,1,0:T(8,128)S(1)}, f32[1,1032,128]{2,1,0:T(8,128)S(1)}, u32[]{:S(2)}, u32[]{:S(2)}) collective-permute-start(f32[1,1032,128]{2,1,0:T(8,128)S(1)} %select_maximum_fusion.4), channel_id=1, source_target_pairs={{0,16},{8,24},{16,0},{24,8},{1,17},{9,25},{17,1},{25,9},{2,18},{10... | collective-permute-start | bytes 1585160 | tf_op jit(solution)/shard_map/ppermute | solution.py:43
  459.7 28.3 %collective-permute-start.8 = (f32[1,1032,128]{2,1,0:T(8,128)S(1)}, f32[1,1032,128]{2,1,0:T(8,128)S(1)}, u32[]{:S(2)}, u32[]{:S(2)}) collective-permute-start(f32[1,1032,128]{2,1,0:T(8,128)S(1)} %select_maximum_fusion.4), channel_id=1, source_target_pairs={{0,8},{8,16},{16,24},{24,0},{1,9},{9,17},{17,25},{25,1},{2,10},{10... | collective-permute-start | bytes 1585160 | tf_op jit(solution)/shard_map/ppermute | solution.py:43
  465.7 35.4 %collective-permute-start.15 = (f32[1,1032,128]{2,1,0:T(8,128)S(1)}, f32[1,1032,128]{2,1,0:T(8,128)S(1)}, u32[]{:S(2)}, u32[]{:S(2)}) collective-permute-start(f32[1,1032,128]{2,1,0:T(8,128)S(1)} %select_maximum_fusion.1), channel_id=1, source_target_pairs={{0,24},{8,0},{16,8},{24,16},{1,25},{9,1},{17,9},{25,17},{2,26},{10... | collective-permute-start | bytes 1585160 | tf_op jit(solution)/shard_map/ppermute | solution.py:43
  466.7 36.4 %collective-permute-start.16 = (f32[1,1032,128]{2,1,0:T(8,128)S(1)}, f32[1,1032,128]{2,1,0:T(8,128)S(1)}, u32[]{:S(2)}, u32[]{:S(2)}) collective-permute-start(f32[1,1032,128]{2,1,0:T(8,128)S(1)} %select_maximum_fusion.1), channel_id=1, source_target_pairs={{0,16},{8,24},{16,0},{24,8},{1,17},{9,25},{17,1},{25,9},{2,18},{10... | collective-permute-start | bytes 1585160 | tf_op jit(solution)/shard_map/ppermute | solution.py:43
  487.1 16.0 %collective-permute-start.17 = (f32[1,1032,128]{2,1,0:T(8,128)S(1)}, f32[1,1032,128]{2,1,0:T(8,128)S(1)}, u32[]{:S(2)}, u32[]{:S(2)}) collective-permute-start(f32[1,1032,128]{2,1,0:T(8,128)S(1)} %select_maximum_fusion.1), channel_id=1, source_target_pairs={{0,8},{8,16},{16,24},{24,0},{1,9},{9,17},{17,25},{25,1},{2,10},{10... | collective-permute-start | bytes 1585160 | tf_op jit(solution)/shard_map/ppermute | solution.py:43
  488.6 17.3 %collective-permute-start.11 = (f32[1,1032,128]{2,1,0:T(8,128)S(1)}, f32[1,1032,128]{2,1,0:T(8,128)S(1)}, u32[]{:S(2)}, u32[]{:S(2)}) collective-permute-start(f32[1,1032,128]{2,1,0:T(8,128)S(1)} %select_maximum_fusion.3), channel_id=1, source_target_pairs={{0,96},{1,97},{2,98},{3,99},{4,100},{5,101},{6,102},{7,103},{8,104... | collective-permute-start | bytes 1585160 | tf_op jit(solution)/shard_map/ppermute | solution.py:43
  489.3 34.2 %collective-permute-start.10 = (f32[1,1032,128]{2,1,0:T(8,128)S(1)}, f32[1,1032,128]{2,1,0:T(8,128)S(1)}, u32[]{:S(2)}, u32[]{:S(2)}) collective-permute-start(f32[1,1032,128]{2,1,0:T(8,128)S(1)} %select_maximum_fusion.3), channel_id=1, source_target_pairs={{0,64},{32,96},{1,65},{33,97},{2,66},{34,98},{3,67},{35,99},{4,68}... | collective-permute-start | bytes 1585160 | tf_op jit(solution)/shard_map/ppermute | solution.py:43
  501.2 26.2 %collective-permute-start.9 = (f32[1,1032,128]{2,1,0:T(8,128)S(1)}, f32[1,1032,128]{2,1,0:T(8,128)S(1)}, u32[]{:S(2)}, u32[]{:S(2)}) collective-permute-start(f32[1,1032,128]{2,1,0:T(8,128)S(1)} %select_maximum_fusion.3), channel_id=1, source_target_pairs={{0,32},{32,64},{64,96},{1,33},{33,65},{65,97},{2,34},{34,66},{66,9... | collective-permute-start | bytes 1585160 | tf_op jit(solution)/shard_map/ppermute | solution.py:43
  503.3 25.3 %copy-start.14 = (f32[6,16,64,128]{3,2,1,0:T(8,128)S(1)}, f32[6,16,64,128]{3,2,1,0:T(8,128)}, u32[]{:S(2)}) copy-start(f32[6,16,64,128]{3,2,1,0:T(8,128)} %fusion.5) | copy-start | bytes 9437188
  503.8 29.8 %collective-permute-start.20 = (f32[1,1032,128]{2,1,0:T(8,128)S(1)}, f32[1,1032,128]{2,1,0:T(8,128)S(1)}, u32[]{:S(2)}, u32[]{:S(2)}) collective-permute-start(f32[1,1032,128]{2,1,0:T(8,128)S(1)} %select_maximum_fusion), channel_id=1, source_target_pairs={{0,96},{1,97},{2,98},{3,99},{4,100},{5,101},{6,102},{7,103},{8,104... | collective-permute-start | bytes 1585160 | tf_op jit(solution)/shard_map/ppermute | solution.py:43
  504.6 29.0 %collective-permute-start.19 = (f32[1,1032,128]{2,1,0:T(8,128)S(1)}, f32[1,1032,128]{2,1,0:T(8,128)S(1)}, u32[]{:S(2)}, u32[]{:S(2)}) collective-permute-start(f32[1,1032,128]{2,1,0:T(8,128)S(1)} %select_maximum_fusion), channel_id=1, source_target_pairs={{0,64},{32,96},{1,65},{33,97},{2,66},{34,98},{3,67},{35,99},{4,68}... | collective-permute-start | bytes 1585160 | tf_op jit(solution)/shard_map/ppermute | solution.py:43
  506.0 29.6 %collective-permute-start.18 = (f32[1,1032,128]{2,1,0:T(8,128)S(1)}, f32[1,1032,128]{2,1,0:T(8,128)S(1)}, u32[]{:S(2)}, u32[]{:S(2)}) collective-permute-start(f32[1,1032,128]{2,1,0:T(8,128)S(1)} %select_maximum_fusion), channel_id=1, source_target_pairs={{0,32},{32,64},{64,96},{1,33},{33,65},{65,97},{2,34},{34,66},{66,9... | collective-permute-start | bytes 1585160 | tf_op jit(solution)/shard_map/ppermute | solution.py:43
  (60 other events, 312.6 us)
